TPU v7x, 512 devices: a whole 4x8x8 slice. The times are simulated.
512 devices in a mesh: req: 64 (over x, z, core), tp: 8 (over y).
Axes of the slice: x: 4, y: 8, z: 8, core: 2. Of those that a mesh axis runs over, the one named last changes fastest.
Arguments:
- residual_input: bfloat16 [8192, 3584], P('req', 'tp'), may hold values from -6 to 6
- new_token_queries: bfloat16 [8192, 4096], P('req', 'tp'), may hold values from -8 to 8
- new_token_keys: bfloat16 [8192, 2048], P('req', 'tp'), may hold values from -8 to 8
- new_token_values: bfloat16 [8192, 2048], P('req', 'tp'), may hold values from -6 to 6
- key_page_pool: bfloat16 [1536, 16, 2048], P('req', None, 'tp'), may hold values from -6 to 6
- value_page_pool: bfloat16 [1536, 16, 2048], P('req', None, 'tp'), may hold values from -6 to 6
- request_page_table: int32 [128, 64], P('req'), may hold values from -1 to 23, as said below
- page_token_length: int32 [128, 64], P('req'), may hold values from 0 to 16, as said below
- request_token_length: int32 [64, 2], P('req'), may hold values from 1 to 96, 128 in all within a row
- request_adapter: int32 [64, 2], P('req'), may hold values from 0 to 63
- adapter_table_row: int32 [64], replicated, may hold values from 0 to 63, each once
- output_weight: bfloat16 [4096, 3584], P('tp'), may hold values from -0.125 to 0.125
- adapter_down_weight: bfloat16 [64, 16, 4096], P('req', None, 'tp'), may hold values from -0.09375 to 0.09375
- adapter_up_weight: bfloat16 [64, 16, 3584], P('req', None, 'tp'), may hold values from -1.5 to 1.5
- norm_scale_row: float32 [3584], P('tp'), may hold values from 0.25 to 1.75
Outputs:
- hidden_out: bfloat16 [8192, 3584], P('req', 'tp')
Inputs may be any that keep to these rules, and one draw needn't show every extreme that they name: request_page_table[q, o] is a page of the pool of owner o (rows o * 24 to o * 24 + 23 of the pools), or -1; so the 2 requests of one index of req take at most 2 pages from one owner, and in every draw the requests of some index of req each take a page from every owner. Requests may share pages. `page_token_length`: 0 exactly where request_page_table is -1; every used page of a request is full but at most one.
All inputs are finite; a program needn't handle non-finite values.
Results may differ from a plain program's by a relative error of at most 0.015.
Values may be sent and summed in bfloat16 or wider, within the bound.
No kernel may reach another device: no remote copies, remote signals or barrier semaphores. Data moves between devices by JAX's collectives and lax.ppermute only.
A program may use at most 64 MiB of HBM per device.

v0:
```python
import jax
import jax.numpy as jnp
from jax import lax
from jax.sharding import PartitionSpec as P

HEAD_SIZE = 256
epsilon = 1e-06
adapter_scale = 2.0
masked_score = -1e30


def attend(query_rows, new_keys, new_values, gathered_keys, gathered_values, usable, owner_request):
    token_count = query_rows.shape[0]
    kv_heads = new_keys.shape[1] // HEAD_SIZE
    group_size = query_rows.shape[1] // new_keys.shape[1]
    requests_here = gathered_keys.shape[0]
    cached_count = gathered_keys.shape[1]
    query_heads = query_rows.reshape(token_count, kv_heads, group_size, HEAD_SIZE)
    past_keys = gathered_keys.reshape(requests_here, cached_count, kv_heads, HEAD_SIZE)
    past_values = gathered_values.reshape(requests_here * cached_count, kv_heads, HEAD_SIZE)
    fresh_keys = new_keys.reshape(token_count, kv_heads, HEAD_SIZE)
    fresh_values = new_values.reshape(token_count, kv_heads, HEAD_SIZE)
    positions = jnp.arange(token_count, dtype=jnp.int32)
    scaling = HEAD_SIZE ** (-0.5)
    past_scores = (
        jnp.einsum("tgqd,rngd->tgqrn", query_heads, past_keys, preferred_element_type=jnp.float32)
        * scaling
    )
    past_mask = usable[None, :, :] & (
        owner_request[:, None, None] == jnp.arange(requests_here, dtype=jnp.int32)[None, :, None]
    )
    past_scores = jnp.where(past_mask[:, None, None, :, :], past_scores, masked_score)
    past_scores = past_scores.reshape(
        token_count, kv_heads, group_size, requests_here * cached_count
    )
    fresh_scores = (
        jnp.einsum("tgqd,ugd->tgqu", query_heads, fresh_keys, preferred_element_type=jnp.float32)
        * scaling
    )
    fresh_mask = (owner_request[:, None] == owner_request[None, :]) & (
        positions[None, :] <= positions[:, None]
    )
    fresh_scores = jnp.where(fresh_mask[:, None, None, :], fresh_scores, masked_score)
    scores = jnp.concatenate([past_scores, fresh_scores], axis=3)
    highest = jnp.max(scores, axis=3, keepdims=True)
    weights = jnp.exp(scores - highest)
    weights = (weights / jnp.sum(weights, axis=3, keepdims=True)).astype(jnp.bfloat16)
    all_values = jnp.concatenate([past_values, fresh_values], axis=0)
    mixed = jnp.einsum("tgqk,kgd->tgqd", weights, all_values, preferred_element_type=jnp.float32)
    return mixed.reshape(token_count, -1).astype(jnp.bfloat16)


def local(
    residual_input,
    new_token_queries,
    new_token_keys,
    new_token_values,
    key_page_pool,
    value_page_pool,
    request_page_table,
    page_token_length,
    request_token_length,
    request_adapter,
    adapter_table_row,
    output_weight,
    adapter_down_weight,
    adapter_up_weight,
    norm_scale_row,
):
    owners = lax.axis_size("req")
    groups = lax.axis_size("tp")
    requests_here = request_page_table.shape[0]
    page_rows = key_page_pool.shape[1]
    token_count = new_token_queries.shape[0]
    width_part = residual_input.shape[1]
    head_cols = key_page_pool.shape[2]
    down_cols = adapter_down_weight.shape[2]
    adapter_pair = jnp.concatenate([adapter_down_weight, adapter_up_weight], axis=2)
    adapters_everywhere = lax.all_gather(adapter_pair, "req", axis=0, tiled=True)
    wanted = lax.all_to_all(request_page_table, "req", split_axis=1, concat_axis=1, tiled=True)
    page_picks = jnp.maximum(wanted, 0)
    kv_pool = jnp.concatenate([key_page_pool, value_page_pool], axis=2)
    kv_out = kv_pool[page_picks]
    kv_back = lax.all_to_all(kv_out, "req", split_axis=1, concat_axis=1, tiled=True)
    kv_back = kv_back.reshape(requests_here, owners * page_rows, 2 * head_cols)
    gathered_keys = kv_back[:, :, :head_cols]
    gathered_values = kv_back[:, :, head_cols:]
    usable = (
        jnp.arange(page_rows, dtype=jnp.int32)[None, None, :] < page_token_length[:, :, None]
    ).reshape(requests_here, owners * page_rows)
    lengths = request_token_length[0]
    positions = jnp.arange(token_count, dtype=jnp.int32)
    ends = jnp.cumsum(lengths)
    owner_request = jnp.sum((positions[:, None] >= ends[None, :]).astype(jnp.int32), axis=1)
    attention = attend(
        new_token_queries,
        new_token_keys,
        new_token_values,
        gathered_keys,
        gathered_values,
        usable,
        owner_request,
    )
    adapters_all = adapter_table_row.shape[0]
    matches = request_adapter[0][:, None] == jnp.arange(adapters_all, dtype=jnp.int32)[None, :]
    chosen_pages = jnp.sum(jnp.where(matches, adapter_table_row[None, :], 0), axis=1)
    rows_here = adapters_everywhere.shape[0]
    picker = (chosen_pages[:, None] == jnp.arange(rows_here, dtype=jnp.int32)[None, :]).astype(
        jnp.bfloat16
    )
    selected = jnp.einsum(
        "rk,kab->rab", picker, adapters_everywhere, preferred_element_type=jnp.float32
    ).astype(jnp.bfloat16)
    adapter_in = selected[:, :, :down_cols]
    adapter_out = selected[:, :, down_cols:]
    rank_size = adapter_in.shape[1]
    selector = (
        owner_request[:, None] == jnp.arange(requests_here, dtype=jnp.int32)[None, :]
    ).astype(jnp.float32)
    selector_half = selector.astype(jnp.bfloat16)
    base_part = jnp.dot(attention, output_weight, preferred_element_type=jnp.float32)
    low_terms = jnp.einsum("tc,rkc->trk", attention, adapter_in, preferred_element_type=jnp.float32)
    low_part = jnp.sum(low_terms * selector[:, :, None], axis=1)
    base_slots = base_part.astype(jnp.bfloat16).reshape(token_count, groups, width_part)
    base_slots = jnp.transpose(base_slots, (1, 0, 2))
    low_slots = jnp.broadcast_to(
        low_part.astype(jnp.bfloat16)[None], (groups, token_count, rank_size)
    )
    pad_cols = -(width_part + rank_size) % 128
    slots = jnp.concatenate(
        [base_slots, low_slots, jnp.zeros((groups, token_count, pad_cols), jnp.bfloat16)], axis=2
    )
    arrived = lax.all_to_all(slots, "tp", split_axis=0, concat_axis=0, tiled=True)
    arrived = arrived.astype(jnp.float32)
    base_local = jnp.sum(arrived[:, :, :width_part], axis=0)
    low_sum = jnp.sum(arrived[:, :, width_part : width_part + rank_size], axis=0)
    rows_masked = (low_sum.astype(jnp.bfloat16)[:, None, :] * selector_half[:, :, None]).reshape(
        token_count, requests_here * rank_size
    )
    projected = base_local + adapter_scale * jnp.dot(
        rows_masked,
        adapter_out.reshape(requests_here * rank_size, width_part),
        preferred_element_type=jnp.float32,
    )
    square_part = jnp.sum(projected * projected, axis=1)
    square_sum = lax.psum(square_part, "tp")
    mean_square = square_sum / (groups * width_part)
    scaled = projected * lax.rsqrt(mean_square + epsilon)[:, None]
    return (residual_input.astype(jnp.float32) + scaled * norm_scale_row).astype(jnp.bfloat16)


def solution(mesh):
    in_specs = (
        P("req", "tp"),
        P("req", "tp"),
        P("req", "tp"),
        P("req", "tp"),
        P("req", None, "tp"),
        P("req", None, "tp"),
        P("req", None),
        P("req", None),
        P("req", None),
        P("req", None),
        P(),
        P("tp", None),
        P("req", None, "tp"),
        P("req", None, "tp"),
        P("tp"),
    )
    out_specs = P("req", "tp")
    return jax.shard_map(local, mesh=mesh, in_specs=in_specs, out_specs=out_specs, check_vma=False)
```

profile of v0, /device:TPU:8, one launch (start us, length us, event | category | flops | bytes accessed | tf_op | source)
XLA Modules:
  0.0 186.8 jit_solution(3870955451242989684)
XLA Ops:
  6.5 0.0 copy-start
  6.5 1.4 copy.88
  8.0 13.8 %all-to-all-start = ((s32[2,64,1]{0,2,1:T(1,128)}), s32[2,64,1]{0,2,1:T(1,128)S(1)}, u32[]{:S(2)}, u32[]{:S(2)}) async-start(s32[2,64,1]{0,2,1:T(1,128)} %copy.88), calls=%async_computation | async-start | bytes 65536 | tf_op jit(solution)/shard_map/all_to_all | solution.py:80
  21.7 0.0 all-gather.2.cloned.1.call-start
  21.8 1.4 pad_maximum_fusion.1
  23.1 0.0 all-gather.2.cloned.1.call-update
  23.2 1.1 pad_maximum_fusion
  24.2 7.0 %all-to-all-done = s32[2,64,1]{0,2,1:T(1,128)S(1)} async-done(((s32[2,64,1]{0,2,1:T(1,128)}), s32[2,64,1]{0,2,1:T(1,128)S(1)}, u32[]{:S(2)}, u32[]{:S(2)}) %all-to-all-start) | async-done | bytes 544 | tf_op jit(solution)/shard_map/all_to_all | solution.py:80
  31.2 0.1 copy.89
  31.3 0.1 reshape.275
  31.4 0.7 gather_fusion
  32.1 1.6 copy.90
  33.7 0.0 copy-start.15
  33.7 0.0 copy-start.12
  33.7 4.8 %all-to-all-start.1 = ((bf16[2,64,16,512]{3,2,0,1:T(8,128)(2,1)}), bf16[2,64,16,512]{3,2,0,1:T(8,128)(2,1)S(1)}, u32[]{:S(2)}, u32[]{:S(2)}) async-start(bf16[2,64,16,512]{3,2,0,1:T(8,128)(2,1)} %copy.90), calls=%async_computation.1 | async-start | bytes 4194304 | tf_op jit(solution)/shard_map/all_to_all | solution.py:84
  38.5 0.0 copy-done.8
  38.5 0.7 copy.92
  39.3 0.0 copy-done.11
  39.3 0.1 lt.27
  39.4 0.1 lt.28
  39.5 0.1 lt.25
  39.6 0.0 copy-done.13
  39.6 0.2 reduce-window.8
  39.7 0.1 pad.2.clone
  39.8 0.1 fusion.30
  39.9 0.0 copy-done.14
  39.9 0.0 copy-done.15
  39.9 0.2 fusion.31
  40.1 0.1 fusion.22
  40.2 0.3 broadcast_and_fusion
  40.6 0.0 copy-done
  40.6 0.9 fusion.38
  41.4 71.5 %all-gather.2.cloned.1.call-done = bf16[64,16,960]{2,1,0:T(8,128)(2,1)} async-done(((bf16[1,16,960]{2,1,0:T(8,128)(2,1)}), bf16[64,16,960]{2,1,0:T(8,128)(2,1)}) %all-gather.2.cloned.1.call-update) | async-done | bytes 1966096 | tf_op jit(solution)/shard_map/all_gather | solution.py:79
  112.9 3.9 %fusion.10 = bf16[2,16,960]{2,0,1:T(2,128)(2,1)S(1)} fusion(bf16[64,16,960]{2,1,0:T(8,128)(2,1)} %all-gather.2.cloned.1.call-done, s32[2]{0:T(128)S(1)} %fusion.31), kind=kOutput, calls=%fused_computation.19 | convolution fusion | flops 3963008 | bytes 2027528 | tf_op jit(solution)/shard_map/rk,kab->rab/dot_general | solution.py:111
  116.8 0.0 all-to-all-done.1
  116.8 0.2 copy.91
  117.0 0.4 copy-done.5
  117.4 1.3 copy-done.1
  118.8 0.1 slice.26
  118.9 1.4 copy.93
  120.3 0.5 copy-done.2
  120.8 1.4 fusion.37
  122.3 0.1 copy.95
  122.4 0.0 copy-start.4
  122.4 0.0 copy-start.9
  122.5 0.7 copy-done.6
  123.2 0.3 fusion.3
  123.5 0.2 copy-done.4
  123.7 0.6 convolution_convert_fusion.1
  124.2 1.5 copy-done.3
  125.7 0.7 convolution_convert_fusion
  126.4 0.6 copy.99
  127.0 0.1 fusion.17
  127.2 1.3 maximum_maximum_fusion
  128.4 6.8 %all-to-all-start.2 = ((bf16[8,128,512]{1,2,0:T(8,128)(2,1)}), bf16[8,128,512]{1,2,0:T(8,128)(2,1)S(1)}, u32[]{:S(2)}, u32[]{:S(2)}) async-start(bf16[8,128,512]{1,2,0:T(8,128)(2,1)} %maximum_maximum_fusion), calls=%async_computation.2 | async-start | bytes 2097152 | tf_op jit(solution)/shard_map/all_to_all | solution.py:133
  135.3 27.7 %all-to-all-done.2 = bf16[8,128,512]{1,2,0:T(8,128)(2,1)S(1)} async-done(((bf16[8,128,512]{1,2,0:T(8,128)(2,1)}), bf16[8,128,512]{1,2,0:T(8,128)(2,1)S(1)}, u32[]{:S(2)}, u32[]{:S(2)}) %all-to-all-start.2) | async-done | bytes 1048608 | tf_op jit(solution)/shard_map/all_to_all | solution.py:133
  162.9 0.1 convert_element_type.79
  163.1 0.0 copy-start.7
  163.1 0.0 copy-start.10
  163.1 0.1 slice_reduce_fusion
  163.2 0.0 slice-done.1
  163.2 0.3 multiply_reduce_fusion
  163.5 15.6 %psum.7 = f32[128]{0:T(128)S(1)} all-reduce(f32[128]{0:T(128)S(1)} %get-tuple-element.12), channel_id=1, replica_groups=mesh['req'=64,'tp'=8] {'tp'}, use_global_device_ids=true, to_apply=%region_10.11 | all-reduce | flops 128 | bytes 1024 | tf_op jit(solution)/shard_map/psum | solution.py:146
  179.1 0.8 add_convert_fusion
  (26 shorter events, 0.1 us)
Async XLA Ops:
  6.5 34.0 %copy-start = (bf16[128,256]{1,0:T(8,128)(2,1)S(1)}, bf16[128,256]{1,0:T(8,128)(2,1)}, u32[]{:S(2)}) copy-start(bf16[128,256]{1,0:T(8,128)(2,1)} %param.17) | copy-start | bytes 196612
  8.0 23.2 %all-to-all-start = ((s32[2,64,1]{0,2,1:T(1,128)}), s32[2,64,1]{0,2,1:T(1,128)S(1)}, u32[]{:S(2)}, u32[]{:S(2)}) async-start(s32[2,64,1]{0,2,1:T(1,128)} %copy.88), calls=%async_computation | async-start | bytes 65536 | tf_op jit(solution)/shard_map/all_to_all | solution.py:80
  21.7 91.2 %all-gather.2.cloned.1.call-start = ((), (), s32[]{:S(2)}) async-start(), calls=%async_computation.3 | async-start | bytes 2129920 | tf_op jit(solution)/shard_map/all_gather | solution.py:79
  33.7 4.9 %copy-start.8 = (bf16[128,256]{1,0:T(8,128)(2,1)S(1)}, bf16[128,256]{1,0:T(8,128)(2,1)}, u32[]{:S(2)}) copy-start(bf16[128,256]{1,0:T(8,128)(2,1)} %param.18) | copy-start | bytes 196612
  33.7 5.6 %copy-start.11 = (s32[2,64]{1,0:T(2,128)S(1)}, s32[2,64]{1,0:T(2,128)}, u32[]{:S(2)}) copy-start(s32[2,64]{1,0:T(2,128)} %param.22) | copy-start | bytes 1540
  33.7 5.9 %copy-start.13 = (s32[1,2]{1,0:T(1,128)S(1)}, s32[1,2]{1,0:T(1,128)}, u32[]{:S(2)}) copy-start(s32[1,2]{1,0:T(1,128)} %param.23) | copy-start | bytes 28
  33.7 6.2 %copy-start.14 = (s32[64]{0:T(128)S(1)}, s32[64]{0:T(128)}, u32[]{:S(2)}) copy-start(s32[64]{0:T(128)} %param.25) | copy-start | bytes 772
  33.7 6.2 %copy-start.15 = (s32[1,2]{1,0:T(1,128)S(1)}, s32[1,2]{1,0:T(1,128)}, u32[]{:S(2)}) copy-start(s32[1,2]{1,0:T(1,128)} %param.24) | copy-start | bytes 28
  33.7 6.9 %copy-start.12 = (bf16[128,512]{1,0:T(8,128)(2,1)S(1)}, bf16[128,512]{1,0:T(8,128)(2,1)}, u32[]{:S(2)}) copy-start(bf16[128,512]{1,0:T(8,128)(2,1)} %param.16) | copy-start | bytes 393220
  33.7 83.1 %all-to-all-start.1 = ((bf16[2,64,16,512]{3,2,0,1:T(8,128)(2,1)}), bf16[2,64,16,512]{3,2,0,1:T(8,128)(2,1)S(1)}, u32[]{:S(2)}, u32[]{:S(2)}) async-start(bf16[2,64,16,512]{3,2,0,1:T(8,128)(2,1)} %copy.90), calls=%async_computation.1 | async-start | bytes 4194304 | tf_op jit(solution)/shard_map/all_to_all | solution.py:84
  116.8 0.6 copy-start.5
  117.4 1.3 copy-start.1
  118.8 2.0 %copy-start.2 = (bf16[2,64,16,512]{3,2,1,0:T(8,128)(2,1)S(1)}, bf16[2,64,16,512]{3,2,1,0:T(8,128)(2,1)}, u32[]{:S(2)}) copy-start(bf16[2,64,16,512]{3,2,1,0:T(8,128)(2,1)} %copy-done.1) | copy-start | bytes 6291460
  122.3 0.9 copy-start.6
  122.4 1.2 copy-start.4
  122.4 1.2 copy-start.9
  123.7 2.0 %copy-start.3 = (bf16[512,3584]{1,0:T(8,128)(2,1)S(1)}, bf16[512,3584]{1,0:T(8,128)(2,1)}, u32[]{:S(2)}) copy-start(bf16[512,3584]{1,0:T(8,128)(2,1)} %param.26) | copy-start | bytes 11010052
  125.7 1.3 slice-start
  128.4 34.5 %all-to-all-start.2 = ((bf16[8,128,512]{1,2,0:T(8,128)(2,1)}), bf16[8,128,512]{1,2,0:T(8,128)(2,1)S(1)}, u32[]{:S(2)}, u32[]{:S(2)}) async-start(bf16[8,128,512]{1,2,0:T(8,128)(2,1)} %maximum_maximum_fusion), calls=%async_computation.2 | async-start | bytes 2097152 | tf_op jit(solution)/shard_map/all_to_all | solution.py:133
  135.3 27.9 %slice-start.1 = ((bf16[2,16,960]{2,0,1:T(2,128)(2,1)}), bf16[2,16,448]{2,0,1:T(2,128)(2,1)S(1)}, s32[]{:S(2)}) async-start(bf16[2,16,960]{2,0,1:T(2,128)(2,1)} %copy-done.5), calls=%async_computation.5 | async-start | bytes 65536 | tf_op jit(solution)/shard_map/slice | solution.py:115
  163.1 16.1 %copy-start.7 = (bf16[128,448]{0,1:T(8,128)(2,1)S(1)}, bf16[128,448]{0,1:T(8,128)(2,1)}, u32[]{:S(2)}) copy-start(bf16[128,448]{0,1:T(8,128)(2,1)} %param.15) | copy-start | bytes 344068
  163.1 16.1 %copy-start.10 = (f32[448]{0:T(512)S(1)}, f32[448]{0:T(512)}, u32[]{:S(2)}) copy-start(f32[448]{0:T(512)} %param.29) | copy-start | bytes 5380
Sparse Core Ops, SparseCore 0:
  25.9 86.9 all-gather.1
where the time goes:
time: 187 us
  waiting for transfers between devices  106 us (57%)
  starting transfers between devices  25.5 us (14%)
  blocking collectives  15.6 us (8%)
  between operations  13.7 us (7%)
  local copies, waits for them, and re-layouts  12.1 us (6%)
  matrix products  7.86 us (4%)
  other arithmetic  5.9 us (3%)
    all_gather x1, waiting for transfers between devices, local(): lax.all_gather(adapter_pair, 'req', axis=0, tiled=True)  71.5 us
    all_to_all x1, waiting for transfers between devices, local(): lax.all_to_all(slots, 'tp', split_axis=0, concat_axis=0, tiled=True)  27.7 us
    psum x1, blocking collectives, local(): square_sum = lax.psum(square_part, 'tp')  15.6 us
    all_to_all x1, starting transfers between devices, local(): lax.all_to_all(request_page_table, 'req', split_axis=1, concat_axis=1, ti...  13.8 us
    all_to_all x1, waiting for transfers between devices, local(): lax.all_to_all(request_page_table, 'req', split_axis=1, concat_axis=1, ti...  6.97 us
    all_to_all x1, starting transfers between devices, local(): lax.all_to_all(slots, 'tp', split_axis=0, concat_axis=0, tiled=True)  6.83 us
    unnamed x33, local copies, waits for them, and re-layouts  5.44 us
    all_to_all x1, starting transfers between devices, local(): lax.all_to_all(kv_out, 'req', split_axis=1, concat_axis=1, tiled=True)  4.84 us
  transfers between devices with their start and end apart: 4, of which 3 were waited for; matrix products, arithmetic and copies ran while one was open for 6% of the time, Pallas kernels for 0%

commit v1 on v0

--- a/solution.py
+++ b/solution.py
@@ -7,6 +7,16 @@
 epsilon = 1e-06
 adapter_scale = 2.0
 masked_score = -1e30
+
+
+def side_enter(xin, which_axis):
+    degree = jax.lax.axis_size(which_axis)
+    taken_in, z1 = (xin, 0)
+    while 1 << z1 < degree:
+        inter = jax.lax.ppermute(taken_in, which_axis, [(ii, ii ^ 1 << z1) for ii in range(degree)])
+        taken_in = taken_in + inter
+        z1 = z1 + 1
+    return taken_in
 
 
 def attend(query_rows, new_keys, new_values, gathered_keys, gathered_values, usable, owner_request):
@@ -143,7 +153,7 @@
         preferred_element_type=jnp.float32,
     )
     square_part = jnp.sum(projected * projected, axis=1)
-    square_sum = lax.psum(square_part, "tp")
+    square_sum = side_enter(square_part, "tp")
     mean_square = square_sum / (groups * width_part)
     scaled = projected * lax.rsqrt(mean_square + epsilon)[:, None]
     return (residual_input.astype(jnp.float32) + scaled * norm_scale_row).astype(jnp.bfloat16)

time: 187 us -> 193 us (1.032)
  the two profiles are of different devices: /device:TPU:8 before, /device:TPU:4 now
where the time goes in v1:
time: 193 us
  waiting for transfers between devices  119 us (62%)
  starting transfers between devices  34.3 us (18%)
  between operations  13.7 us (7%)
  local copies, waits for them, and re-layouts  12.1 us (6%)
  matrix products  7.86 us (4%)
  other arithmetic  5.89 us (3%)
    all_gather x1, waiting for transfers between devices, local(): lax.all_gather(adapter_pair, 'req', axis=0, tiled=True)  70.1 us
    all_to_all x1, waiting for transfers between devices, local(): lax.all_to_all(slots, 'tp', split_axis=0, concat_axis=0, tiled=True)  29.2 us
    ppermute x3, waiting for transfers between devices, side_enter(): jax.lax.ppermute(taken_in, which_axis, [(ii, ii ^ 1 << z1) for ii in rang...  14.2 us
    all_to_all x1, starting transfers between devices, local(): lax.all_to_all(request_page_table, 'req', split_axis=1, concat_axis=1, ti...  13.9 us
    ppermute x3, starting transfers between devices, side_enter(): jax.lax.ppermute(taken_in, which_axis, [(ii, ii ^ 1 << z1) for ii in rang...  6.99 us
    all_to_all x1, starting transfers between devices, local(): lax.all_to_all(slots, 'tp', split_axis=0, concat_axis=0, tiled=True)  6.72 us
    all_to_all x1, starting transfers between devices, local(): lax.all_to_all(kv_out, 'req', split_axis=1, concat_axis=1, tiled=True)  6.64 us
    unnamed x33, local copies, waits for them, and re-layouts  5.44 us
  transfers between devices with their start and end apart: 7, of which 6 were waited for; matrix products, arithmetic and copies ran while one was open for 6% of the time, Pallas kernels for 0%

profile of v1, /device:TPU:4, one launch (start us, length us, event | category | flops | bytes accessed | tf_op | source)
XLA Modules:
  0.0 192.5 jit_solution(12697119440369508188)
XLA Ops:
  6.5 1.4 copy.88
  8.0 13.9 %all-to-all-start = ((s32[2,64,1]{0,2,1:T(1,128)}), s32[2,64,1]{0,2,1:T(1,128)S(1)}, u32[]{:S(2)}, u32[]{:S(2)}) async-start(s32[2,64,1]{0,2,1:T(1,128)} %copy.88), calls=%async_computation | async-start | bytes 65536 | tf_op jit(solution)/shard_map/all_to_all | solution.py:90
  21.9 0.0 all-gather.2.cloned.1.call-start
  21.9 1.4 pad_maximum_fusion.1
  23.3 0.0 all-gather.2.cloned.1.call-update
  23.3 1.1 pad_maximum_fusion
  24.4 5.2 %all-to-all-done = s32[2,64,1]{0,2,1:T(1,128)S(1)} async-done(((s32[2,64,1]{0,2,1:T(1,128)}), s32[2,64,1]{0,2,1:T(1,128)S(1)}, u32[]{:S(2)}, u32[]{:S(2)}) %all-to-all-start) | async-done | bytes 544 | tf_op jit(solution)/shard_map/all_to_all | solution.py:90
  29.5 0.1 copy.89
  29.6 0.1 reshape.275
  29.7 0.7 gather_fusion
  30.4 1.6 copy.90
  32.0 0.0 copy-start.15
  32.0 0.0 copy-start.12
  32.0 6.6 %all-to-all-start.1 = ((bf16[2,64,16,512]{3,2,0,1:T(8,128)(2,1)}), bf16[2,64,16,512]{3,2,0,1:T(8,128)(2,1)S(1)}, u32[]{:S(2)}, u32[]{:S(2)}) async-start(bf16[2,64,16,512]{3,2,0,1:T(8,128)(2,1)} %copy.90), calls=%async_computation.1 | async-start | bytes 4194304 | tf_op jit(solution)/shard_map/all_to_all | solution.py:94
  38.7 0.7 copy.92
  39.4 0.1 lt.27
  39.5 0.1 lt.28
  39.6 0.1 lt.25
  39.7 0.2 reduce-window.8
  39.9 0.1 pad.2.clone
  40.0 0.1 fusion.30
  40.1 0.0 copy-done.15
  40.1 0.2 fusion.31
  40.3 0.1 fusion.22
  40.4 0.3 broadcast_and_fusion
  40.7 0.0 copy-done
  40.7 0.0 copy-done.12
  40.7 0.8 fusion.38
  41.6 70.1 %all-gather.2.cloned.1.call-done = bf16[64,16,960]{2,1,0:T(8,128)(2,1)} async-done(((bf16[1,16,960]{2,1,0:T(8,128)(2,1)}), bf16[64,16,960]{2,1,0:T(8,128)(2,1)}) %all-gather.2.cloned.1.call-update) | async-done | bytes 1966096 | tf_op jit(solution)/shard_map/all_gather | solution.py:89
  111.7 3.9 %fusion.10 = bf16[2,16,960]{2,0,1:T(2,128)(2,1)S(1)} fusion(bf16[64,16,960]{2,1,0:T(8,128)(2,1)} %all-gather.2.cloned.1.call-done, s32[2]{0:T(128)S(1)} %fusion.31), kind=kOutput, calls=%fused_computation.19 | convolution fusion | flops 3963008 | bytes 2027528 | tf_op jit(solution)/shard_map/rk,kab->rab/dot_general | solution.py:121
  115.6 0.0 all-to-all-done.1
  115.6 0.2 copy.91
  115.8 0.4 copy-done.5
  116.2 1.4 copy-done.1
  117.6 0.1 slice.26
  117.7 1.4 copy.93
  119.1 0.5 copy-done.2
  119.6 1.5 fusion.37
  121.1 0.1 copy.95
  121.2 0.0 copy-start.9
  121.3 0.7 copy-done.6
  122.0 0.3 fusion.3
  122.3 0.2 copy-done.4
  122.5 0.6 convolution_convert_fusion.1
  123.1 1.5 copy-done.3
  124.5 0.7 convolution_convert_fusion
  125.2 0.6 copy.99
  125.8 0.1 fusion.17
  126.0 1.2 maximum_maximum_fusion
  127.2 6.7 %all-to-all-start.2 = ((bf16[8,128,512]{1,2,0:T(8,128)(2,1)}), bf16[8,128,512]{1,2,0:T(8,128)(2,1)S(1)}, u32[]{:S(2)}, u32[]{:S(2)}) async-start(bf16[8,128,512]{1,2,0:T(8,128)(2,1)} %maximum_maximum_fusion), calls=%async_computation.2 | async-start | bytes 2097152 | tf_op jit(solution)/shard_map/all_to_all | solution.py:143
  134.0 29.2 %all-to-all-done.2 = bf16[8,128,512]{1,2,0:T(8,128)(2,1)S(1)} async-done(((bf16[8,128,512]{1,2,0:T(8,128)(2,1)}), bf16[8,128,512]{1,2,0:T(8,128)(2,1)S(1)}, u32[]{:S(2)}, u32[]{:S(2)}) %all-to-all-start.2) | async-done | bytes 1048608 | tf_op jit(solution)/shard_map/all_to_all | solution.py:143
  163.1 0.1 convert_element_type.79
  163.3 0.0 copy-start.7
  163.3 0.0 copy-start.10
  163.3 0.1 slice_reduce_fusion
  163.4 0.3 multiply_reduce_fusion
  163.7 2.4 %collective-permute-start = (f32[128]{0:T(128)S(1)}, f32[128]{0:T(128)S(1)}, u32[]{:S(2)}, u32[]{:S(2)}) collective-permute-start(f32[128]{0:T(128)S(1)} %get-tuple-element.12), channel_id=1, source_target_pairs={{0,1},{1,0},{2,3},{3,2},{4,5},{5,4},{6,7},{7,6},{8,9},{9,8},{10,11... | collective-permute-start | bytes 1544 | tf_op jit(solution)/shard_map/ppermute | solution.py:16
  166.1 3.0 %collective-permute-done = f32[128]{0:T(128)S(1)} collective-permute-done((f32[128]{0:T(128)S(1)}, f32[128]{0:T(128)S(1)}, u32[]{:S(2)}, u32[]{:S(2)}) %collective-permute-start) | collective-permute-done | bytes 544 | tf_op jit(solution)/shard_map/ppermute | solution.py:16
  169.1 2.1 %collective-permute-start.1 = (f32[128]{0:T(128)S(1)}, f32[128]{0:T(128)S(1)}, u32[]{:S(2)}, u32[]{:S(2)}) collective-permute-start(f32[128]{0:T(128)S(1)} %add.24), channel_id=1, source_target_pairs={{0,2},{1,3},{2,0},{3,1},{4,6},{5,7},{6,4},{7,5},{8,10},{9,11},{10,... | collective-permute-start | bytes 1544 | tf_op jit(solution)/shard_map/ppermute | solution.py:16
  171.3 4.2 %collective-permute-done.1 = f32[128]{0:T(128)S(1)} collective-permute-done((f32[128]{0:T(128)S(1)}, f32[128]{0:T(128)S(1)}, u32[]{:S(2)}, u32[]{:S(2)}) %collective-permute-start.1) | collective-permute-done | bytes 544 | tf_op jit(solution)/shard_map/ppermute | solution.py:16
  175.5 2.4 %collective-permute-start.2 = (f32[128]{0:T(128)S(1)}, f32[128]{0:T(128)S(1)}, u32[]{:S(2)}, u32[]{:S(2)}) collective-permute-start(f32[128]{0:T(128)S(1)} %add.25), channel_id=1, source_target_pairs={{0,4},{1,5},{2,6},{3,7},{4,0},{5,1},{6,2},{7,3},{8,12},{9,13},{10,... | collective-permute-start | bytes 1544 | tf_op jit(solution)/shard_map/ppermute | solution.py:16
  177.9 6.9 %collective-permute-done.2 = f32[128]{0:T(128)S(1)} collective-permute-done((f32[128]{0:T(128)S(1)}, f32[128]{0:T(128)S(1)}, u32[]{:S(2)}, u32[]{:S(2)}) %collective-permute-start.2) | collective-permute-done | bytes 544 | tf_op jit(solution)/shard_map/ppermute | solution.py:16
  184.9 0.0 copy-done.7
  184.9 0.8 add_convert_fusion
  (33 shorter events, 0.1 us)
Async XLA Ops:
  6.5 34.2 %copy-start = (bf16[128,256]{1,0:T(8,128)(2,1)S(1)}, bf16[128,256]{1,0:T(8,128)(2,1)}, u32[]{:S(2)}) copy-start(bf16[128,256]{1,0:T(8,128)(2,1)} %param.17) | copy-start | bytes 196612
  8.0 21.6 %all-to-all-start = ((s32[2,64,1]{0,2,1:T(1,128)}), s32[2,64,1]{0,2,1:T(1,128)S(1)}, u32[]{:S(2)}, u32[]{:S(2)}) async-start(s32[2,64,1]{0,2,1:T(1,128)} %copy.88), calls=%async_computation | async-start | bytes 65536 | tf_op jit(solution)/shard_map/all_to_all | solution.py:90
  21.9 89.8 %all-gather.2.cloned.1.call-start = ((), (), s32[]{:S(2)}) async-start(), calls=%async_computation.3 | async-start | bytes 2129920 | tf_op jit(solution)/shard_map/all_gather | solution.py:89
  32.0 6.7 %copy-start.8 = (bf16[128,256]{1,0:T(8,128)(2,1)S(1)}, bf16[128,256]{1,0:T(8,128)(2,1)}, u32[]{:S(2)}) copy-start(bf16[128,256]{1,0:T(8,128)(2,1)} %param.18) | copy-start | bytes 196612
  32.0 7.4 %copy-start.11 = (s32[2,64]{1,0:T(2,128)S(1)}, s32[2,64]{1,0:T(2,128)}, u32[]{:S(2)}) copy-start(s32[2,64]{1,0:T(2,128)} %param.22) | copy-start | bytes 1540
  32.0 7.7 %copy-start.13 = (s32[1,2]{1,0:T(1,128)S(1)}, s32[1,2]{1,0:T(1,128)}, u32[]{:S(2)}) copy-start(s32[1,2]{1,0:T(1,128)} %param.23) | copy-start | bytes 28
  32.0 8.0 %copy-start.14 = (s32[64]{0:T(128)S(1)}, s32[64]{0:T(128)}, u32[]{:S(2)}) copy-start(s32[64]{0:T(128)} %param.25) | copy-start | bytes 772
  32.0 8.0 %copy-start.15 = (s32[1,2]{1,0:T(1,128)S(1)}, s32[1,2]{1,0:T(1,128)}, u32[]{:S(2)}) copy-start(s32[1,2]{1,0:T(1,128)} %param.24) | copy-start | bytes 28
  32.0 8.7 %copy-start.12 = (bf16[128,512]{1,0:T(8,128)(2,1)S(1)}, bf16[128,512]{1,0:T(8,128)(2,1)}, u32[]{:S(2)}) copy-start(bf16[128,512]{1,0:T(8,128)(2,1)} %param.16) | copy-start | bytes 393220
  32.0 83.6 %all-to-all-start.1 = ((bf16[2,64,16,512]{3,2,0,1:T(8,128)(2,1)}), bf16[2,64,16,512]{3,2,0,1:T(8,128)(2,1)S(1)}, u32[]{:S(2)}, u32[]{:S(2)}) async-start(bf16[2,64,16,512]{3,2,0,1:T(8,128)(2,1)} %copy.90), calls=%async_computation.1 | async-start | bytes 4194304 | tf_op jit(solution)/shard_map/all_to_all | solution.py:94
  115.6 0.6 copy-start.5
  116.2 1.4 copy-start.1
  117.7 2.0 %copy-start.2 = (bf16[2,64,16,512]{3,2,1,0:T(8,128)(2,1)S(1)}, bf16[2,64,16,512]{3,2,1,0:T(8,128)(2,1)}, u32[]{:S(2)}) copy-start(bf16[2,64,16,512]{3,2,1,0:T(8,128)(2,1)} %copy-done.1) | copy-start | bytes 6291460
  121.1 0.9 copy-start.6
  121.2 1.2 copy-start.4
  121.2 1.2 copy-start.9
  122.5 2.0 %copy-start.3 = (bf16[512,3584]{1,0:T(8,128)(2,1)S(1)}, bf16[512,3584]{1,0:T(8,128)(2,1)}, u32[]{:S(2)}) copy-start(bf16[512,3584]{1,0:T(8,128)(2,1)} %param.26) | copy-start | bytes 11010052
  124.5 1.3 slice-start
  127.2 35.9 %all-to-all-start.2 = ((bf16[8,128,512]{1,2,0:T(8,128)(2,1)}), bf16[8,128,512]{1,2,0:T(8,128)(2,1)S(1)}, u32[]{:S(2)}, u32[]{:S(2)}) async-start(bf16[8,128,512]{1,2,0:T(8,128)(2,1)} %maximum_maximum_fusion), calls=%async_computation.2 | async-start | bytes 2097152 | tf_op jit(solution)/shard_map/all_to_all | solution.py:143
  134.0 29.4 %slice-start.1 = ((bf16[2,16,960]{2,0,1:T(2,128)(2,1)}), bf16[2,16,448]{2,0,1:T(2,128)(2,1)S(1)}, s32[]{:S(2)}) async-start(bf16[2,16,960]{2,0,1:T(2,128)(2,1)} %copy-done.5), calls=%async_computation.5 | async-start | bytes 65536 | tf_op jit(solution)/shard_map/slice | solution.py:125
  163.3 21.6 %copy-start.7 = (bf16[128,448]{0,1:T(8,128)(2,1)S(1)}, bf16[128,448]{0,1:T(8,128)(2,1)}, u32[]{:S(2)}) copy-start(bf16[128,448]{0,1:T(8,128)(2,1)} %param.15) | copy-start | bytes 344068
  163.3 21.6 %copy-start.10 = (f32[448]{0:T(512)S(1)}, f32[448]{0:T(512)}, u32[]{:S(2)}) copy-start(f32[448]{0:T(512)} %param.29) | copy-start | bytes 5380
  163.7 5.5 %collective-permute-start = (f32[128]{0:T(128)S(1)}, f32[128]{0:T(128)S(1)}, u32[]{:S(2)}, u32[]{:S(2)}) collective-permute-start(f32[128]{0:T(128)S(1)} %get-tuple-element.12), channel_id=1, source_target_pairs={{0,1},{1,0},{2,3},{3,2},{4,5},{5,4},{6,7},{7,6},{8,9},{9,8},{10,11... | collective-permute-start | bytes 1544 | tf_op jit(solution)/shard_map/ppermute | solution.py:16
  169.1 6.3 %collective-permute-start.1 = (f32[128]{0:T(128)S(1)}, f32[128]{0:T(128)S(1)}, u32[]{:S(2)}, u32[]{:S(2)}) collective-permute-start(f32[128]{0:T(128)S(1)} %add.24), channel_id=1, source_target_pairs={{0,2},{1,3},{2,0},{3,1},{4,6},{5,7},{6,4},{7,5},{8,10},{9,11},{10,... | collective-permute-start | bytes 1544 | tf_op jit(solution)/shard_map/ppermute | solution.py:16
  175.5 9.4 %collective-permute-start.2 = (f32[128]{0:T(128)S(1)}, f32[128]{0:T(128)S(1)}, u32[]{:S(2)}, u32[]{:S(2)}) collective-permute-start(f32[128]{0:T(128)S(1)} %add.25), channel_id=1, source_target_pairs={{0,4},{1,5},{2,6},{3,7},{4,0},{5,1},{6,2},{7,3},{8,12},{9,13},{10,... | collective-permute-start | bytes 1544 | tf_op jit(solution)/shard_map/ppermute | solution.py:16
Sparse Core Ops, SparseCore 0:
  26.1 85.5 all-gather.1
